TPU v7x, 32 devices: a whole 2x2x4 slice. The times are simulated.
32 devices in a mesh: shard: 4 (over z), rep: 8 (over y, x, core).
Axes of the slice: x: 2, y: 2, z: 4, core: 2. Of those that a mesh axis runs over, the one named last changes fastest.
Arguments:
- grads: bfloat16 [1, 8192, 28672], P(None, 'shard', 'rep'), may hold values from -81 to 81
- seeds: int32 [1], replicated, may hold values from 0 to 999999
Outputs:
- projected: bfloat16 [512, 1, 28672], P('shard', None, 'rep')
All inputs are finite; a program needn't handle non-finite values.
Results may differ from a plain program's by a relative error of at most 0.0056.
Values may be sent and summed in bfloat16 or wider, within the bound.
No kernel may reach another device: no remote copies, remote signals or barrier semaphores. Data moves between devices by JAX's collectives and lax.ppermute only.
A program may use at most 128 MiB of HBM per device.

v0:
```python
import jax
import jax.numpy as jnp
from jax import lax
from jax.sharding import PartitionSpec as P

RANK = 512
mix_first = 668265263
mix_second = -2048144789
mix_third = -1028477387


def sketch_table(seeds, first_row, count, rank):
    rows = first_row + lax.iota(jnp.int32, count)
    columns = lax.iota(jnp.int32, rank)
    counter = rows[:, None] * jnp.int32(rank) + columns[None, :]
    hashed = jnp.bitwise_xor(counter[None, :, :], (seeds * jnp.int32(mix_first))[:, None, None])
    hashed = hashed * jnp.int32(mix_second)
    hashed = jnp.bitwise_xor(hashed, lax.shift_right_logical(hashed, jnp.int32(15)))
    hashed = hashed * jnp.int32(mix_third)
    hashed = jnp.bitwise_xor(hashed, lax.shift_right_logical(hashed, jnp.int32(13)))
    unit = lax.shift_right_logical(hashed, jnp.int32(8)).astype(jnp.float32) * (1.0 / 16777216.0)
    return (2.0 * unit - 1.0).astype(jnp.bfloat16)


def body(grads, seeds):
    mats, depth, width = grads.shape
    col0 = lax.axis_index("rep") * width
    outs = []
    for m in range(mats):
        table = sketch_table(seeds[m : m + 1], col0, width, RANK)[0]
        g = grads[m]
        partial = jnp.dot(g, table, preferred_element_type=jnp.float32)
        sketch_rows = lax.psum(partial, "rep")
        local_gram = jnp.dot(
            sketch_rows.T,
            sketch_rows,
            precision=lax.Precision.HIGHEST,
            preferred_element_type=jnp.float32,
        )
        gram = lax.psum(local_gram, "shard")
        factor = jnp.linalg.cholesky(gram)
        basis_rows = lax.linalg.triangular_solve(
            factor, sketch_rows, left_side=False, lower=True, transpose_a=True
        ).astype(jnp.bfloat16)
        partial_sum = jnp.dot(basis_rows.T, g, preferred_element_type=jnp.float32)
        outs.append(partial_sum)
    partial_sum = jnp.stack(outs, axis=1).astype(jnp.bfloat16)
    return lax.psum_scatter(partial_sum, "shard", scatter_dimension=0, tiled=True)


def solution(mesh):
    return jax.shard_map(
        body,
        mesh=mesh,
        in_specs=(P(None, "shard", "rep"), P()),
        out_specs=P("shard", None, "rep"),
        check_vma=False,
    )
```

profile of v0, /device:TPU:0, one launch (start us, length us, event | category | flops | bytes accessed | tf_op | source)
XLA Modules:
  0.0 411.4 jit_solution(13956208684615322948)
XLA Ops:
  6.5 0.0 all-reduce.4.cloned.1.call-start
  7.2 16.7 %fusion.27 = f32[2048,512]{0,1:T(8,128)} fusion(bf16[1,2048,3584]{2,1,0:T(8,128)(2,1)} %param.2, s32[]{:T(128)} %bitcast, s32[3584]{0:T(1024)S(1)} %add_multiply_fusion), kind=kOutput, calls=%fused_computation.26 | convolution fusion | flops 7540047872 | bytes 18888708 | tf_op jit(solution)/shard_map/dot_general | solution.py:32
  23.9 0.0 all-reduce.4.cloned.1.call-update
  23.9 0.3 all-reduce.6.cloned.1.call-start
  24.3 83.4 %all-reduce.4.cloned.1.call-done = f32[2048,512]{0,1:T(8,128)} async-done(((f32[2048,512]{0,1:T(8,128)}), f32[2048,512]{0,1:T(8,128)}) %all-reduce.4.cloned.1.call-update) | async-done | bytes 4194320 | tf_op jit(solution)/shard_map/psum | solution.py:33
  107.6 10.2 %fusion.84 = f32[512,512]{0,1:T(8,128)} fusion(f32[2048,512]{0,1:T(8,128)} %all-reduce.4.cloned.1.call-done), kind=kOutput, calls=%fused_computation.111 | convolution fusion | flops 6442450944 | bytes 5242880 | tf_op jit(solution)/shard_map/dot_general | solution.py:34
  117.9 0.0 all-reduce.6.cloned.1.call-update
  117.9 0.0 reduce-scatter.2.cloned.1.call-start
  118.0 52.0 %all-reduce.6.cloned.1.call-done = f32[512,512]{0,1:T(8,128)} async-done(((f32[512,512]{0,1:T(8,128)}), f32[512,512]{0,1:T(8,128)}) %all-reduce.6.cloned.1.call-update) | async-done | bytes 1048592 | tf_op jit(solution)/shard_map/psum | solution.py:40
  170.0 1.6 copy.6
  171.6 1.4 fusion.53
  173.0 11.7 %cholesky.104 = f32[128,128]{1,0:T(8,128)S(1)} custom-call(f32[128,128]{1,0:T(8,128)S(1)} %cholesky.266), custom_call_target="Cholesky" | custom-call | tf_op jit(solution)/shard_map/jit(cholesky)/cholesky | solution.py:41
  184.8 9.8 %custom-call.30 = f32[1,128,128]{1,2,0:T(8,128)S(1)} custom-call(f32[1,128,128]{2,1,0:T(8,128)S(1)} %get-tuple-element.32), custom_call_target="InvertDiagBlocksLowerTriangular" | custom-call | tf_op jit(solution)/shard_map/jit(cholesky)/cholesky | solution.py:41
  194.6 0.1 cholesky.224
  194.7 0.3 constant_dynamic-update-slice_fusion.3
  195.1 0.3 convolution_subtract_fusion.2
  195.4 11.7 %cholesky.217 = f32[128,128]{1,0:T(8,128)S(1)} custom-call(f32[128,128]{1,0:T(8,128)S(1)} %cholesky.270), custom_call_target="Cholesky" | custom-call | tf_op jit(solution)/shard_map/jit(cholesky)/cholesky | solution.py:41
  207.2 18.5 %custom-call.31 = f32[1,128,128]{1,2,0:T(8,128)S(1)} custom-call(f32[1,128,128]{2,1,0:T(8,128)S(1)} %get-tuple-element.29), custom_call_target="InvertDiagBlocksLowerTriangular" | custom-call | tf_op jit(solution)/shard_map/jit(cholesky)/cholesky | solution.py:41
  225.7 0.3 convolution_dynamic-update-slice_fusion
  225.9 0.4 convolution_subtract_fusion.3
  226.3 11.7 %cholesky.238 = f32[128,128]{1,0:T(8,128)S(1)} custom-call(f32[128,128]{1,0:T(8,128)S(1)} %cholesky.275), custom_call_target="Cholesky" | custom-call | tf_op jit(solution)/shard_map/jit(cholesky)/cholesky | solution.py:41
  238.1 0.7 compare_reduce_fusion.1
  238.7 9.8 %custom-call.32 = f32[1,128,128]{1,2,0:T(8,128)S(1)} custom-call(f32[1,128,128]{2,1,0:T(8,128)S(1)} %get-tuple-element.26), custom_call_target="InvertDiagBlocksLowerTriangular" | custom-call | tf_op jit(solution)/shard_map/jit(cholesky)/cholesky | solution.py:41
  248.6 0.2 convolution_dynamic-update-slice_fusion.1
  248.8 0.4 convolution_subtract_fusion.4
  249.2 11.7 %cholesky.255 = f32[128,128]{1,0:T(8,128)S(1)} custom-call(f32[128,128]{1,0:T(8,128)S(1)} %convolution_subtract_fusion.4), custom_call_target="Cholesky" | custom-call | tf_op jit(solution)/shard_map/jit(cholesky)/cholesky | solution.py:41
  260.9 0.7 compare_reduce_fusion
  261.6 0.7 compare_reduce_fusion.2
  264.8 0.3 select_select_fusion
  265.1 7.8 %while.1 = (s32[]{:T(128)}, f32[512,512]{1,0:T(8,128)S(1)}, s32[4,2]{0,1:T(2,128)S(1)}, f32[4,128,128]{2,1,0:T(8,128)S(1)}, s32[]{:T(128)}) while((s32[]{:T(128)}, f32[512,512]{1,0:T(8,128)S(1)}, s32[4,2]{0,1:T(2,128)S(1)}, f32[4,128,128]{2,1,0:T(8,128)S(1)}, s32[]{:T(128)}) %tuple.30), condition=%wide.while_cond, body=%wide.while_body.sunk | while | flops 2 | bytes 131189 | solution.py:42
  265.2 0.1 constant_dynamic-slice_fusion.2
  265.2 0.5 fusion.93
  265.8 1.3 bitcast_dynamic-update-slice_fusion.2
  267.1 0.1 constant_dynamic-slice_fusion.2
  267.2 0.5 fusion.93
  267.7 1.3 bitcast_dynamic-update-slice_fusion.2
  269.1 0.1 constant_dynamic-slice_fusion.2
  269.1 0.5 fusion.93
  269.7 1.3 bitcast_dynamic-update-slice_fusion.2
  271.0 0.1 constant_dynamic-slice_fusion.2
  271.1 0.5 fusion.93
  271.6 1.3 bitcast_dynamic-update-slice_fusion.2
  273.0 39.3 %custom-call.33 = f32[4,128,128]{1,2,0:T(8,128)S(1)} custom-call(f32[4,128,128]{2,1,0:T(8,128)S(1)} %get-tuple-element.12), custom_call_target="InvertDiagBlocksLowerTriangular" | custom-call | tf_op jit(solution)/shard_map/triangular_solve | solution.py:42
  312.3 0.0 copy-start
  312.3 2.5 fusion.83
  314.8 2.3 convolution_subtract_fusion.1
  317.1 1.1 fusion.82
  318.2 0.0 copy-done
  318.2 1.3 convolution_subtract_fusion
  319.5 1.1 fusion.81
  320.6 2.2 fusion.38
  322.8 1.1 convolution_convert_fusion
  323.9 12.6 %fusion.13 = bf16[512,1,3584]{2,0,1:T(8,128)(2,1)} fusion(bf16[1,2048,3584]{2,1,0:T(8,128)(2,1)} %param.2, bf16[2048,128]{0,1:T(8,128)(2,1)S(1)} %convolution_convert_fusion, bf16[2048,128]{0,1:T(8,128)(2,1)S(1)} %get-tuple-element.35, bf16[2048,128]{0,1:T(8,128)(2,1)S(1)} %get-tuple-element.37, bf16[2048,128]{0,1:T(8,128)(2,1)S(1)} %get-tuple-element.39), kind=kOutput, calls=%fused_computation.15 | convolution fusion | flops 7526416384 | bytes 20447232 | tf_op jit(solution)/shard_map/dot_general | solution.py:45
  336.5 0.0 reduce-scatter.2.cloned.1.call-update
  336.5 68.0 %reduce-scatter.2.cloned.1.call-done = bf16[128,1,3584]{2,0,1:T(8,128)(2,1)} async-done(((bf16[512,1,3584]{2,0,1:T(8,128)(2,1)}), bf16[128,1,3584]{2,0,1:T(8,128)(2,1)}) %reduce-scatter.2.cloned.1.call-update) | async-done | bytes 917520 | tf_op jit(solution)/shard_map/reduce_scatter | solution.py:48
  (11 shorter events, 0.2 us)
Async XLA Ops:
  6.5 101.1 %all-reduce.4.cloned.1.call-start = ((), (), s32[]{:S(2)}) async-start(), calls=%async_computation.1 | async-start | bytes 8388608 | tf_op jit(solution)/shard_map/psum | solution.py:33
  23.9 146.1 %all-reduce.6.cloned.1.call-start = ((), (), s32[]{:S(2)}) async-start(), calls=%async_computation.2 | async-start | bytes 2097152 | tf_op jit(solution)/shard_map/psum | solution.py:40
  117.9 286.6 %reduce-scatter.2.cloned.1.call-start = ((), (), s32[]{:S(2)}) async-start(), calls=%async_computation.3 | async-start | bytes 4587520 | tf_op jit(solution)/shard_map/reduce_scatter | solution.py:48
  312.3 5.9 %copy-start = (f32[2048,512]{0,1:T(8,128)S(1)}, f32[2048,512]{0,1:T(8,128)}, u32[]{:S(2)}) copy-start(f32[2048,512]{0,1:T(8,128)} %all-reduce.4.cloned.1.call-done) | copy-start | bytes 12582916
Sparse Core Ops, SparseCore 0:
  24.1 83.5 all-reduce.3
  118.0 51.9 all-reduce.5
  336.6 67.8 reduce-scatter.1
where the time goes:
time: 419 us; the launch traced here: 411 us
  waiting for transfers between devices  203 us (48%)
  other arithmetic  128 us (31%)
  matrix products  52.9 us (13%)
  between operations  16.9 us (4%)
  local copies, waits for them, and re-layouts  9.44 us (2%)
    another operation x14, other arithmetic, body(): factor = jnp.linalg.cholesky(gram)  87.2 us
    psum x1, waiting for transfers between devices, body(): sketch_rows = lax.psum(partial, 'rep')  83.4 us
    reduce_scatter x1, waiting for transfers between devices, body(): lax.psum_scatter(partial_sum, 'shard', scatter_dimension=0, tiled=True)  68 us
    psum x1, waiting for transfers between devices, body(): gram = lax.psum(local_gram, 'shard')  52 us
    another operation x3, other arithmetic, body(): lax.linalg.triangular_solve(factor, sketch_rows, left_side=False, lower=T...  39.7 us
    dot_general x1, matrix products, body(): partial = jnp.dot(g, table, preferred_element_type=jnp.float32)  16.7 us
    dot_general x1, matrix products, body(): partial_sum = jnp.dot(basis_rows.T, g, preferred_element_type=jnp.float32)  12.6 us
    another operation x7, matrix products, body(): lax.linalg.triangular_solve(factor, sketch_rows, left_side=False, lower=T...  11.5 us
  transfers between devices with their start and end apart: 3, of which 3 were waited for; matrix products, arithmetic and copies ran while one was open for 0% of the time, Pallas kernels for 0%

commit v1 on v0

--- a/solution.py
+++ b/solution.py
@@ -7,6 +7,11 @@
 mix_first = 668265263
 mix_second = -2048144789
 mix_third = -1028477387
+
+
+def summed_here(x, axis):
+    pieces = lax.all_gather(x, axis)
+    return jnp.sum(pieces, axis=0)
 
 
 def sketch_table(seeds, first_row, count, rank):
@@ -30,7 +35,7 @@
         table = sketch_table(seeds[m : m + 1], col0, width, RANK)[0]
         g = grads[m]
         partial = jnp.dot(g, table, preferred_element_type=jnp.float32)
-        sketch_rows = lax.psum(partial, "rep")
+        sketch_rows = summed_here(partial, "rep")
         local_gram = jnp.dot(
             sketch_rows.T,
             sketch_rows,

time: 419 us -> 556 us (1.33)
  waiting for transfers between devices: 203 us -> 277 us
  local copies, waits for them, and re-layouts: 9.44 us -> 55.2 us
  matrix products: 52.9 us -> 64.2 us
  other arithmetic: 128 us -> 134 us
    all_gather x0 -> x1, waiting for transfers between devices: none -> 163 us  [summed_here(): pieces = lax.all_gather(x, axis)]
    psum x1 -> x0, waiting for transfers between devices: 83.4 us -> none  [body(): sketch_rows = lax.psum(partial, 'rep')]
    unnamed x2 -> x8, local copies, waits for them, and re-layouts: 0.01 us -> 36.7 us
    reduce_sum x0 -> x1, other arithmetic: none -> 12.7 us  [summed_here(): return jnp.sum(pieces, axis=0)]
    another operation x14, other arithmetic: 87.2 us -> 78.8 us  [body(): factor = jnp.linalg.cholesky(gram)]
    another operation x7, matrix products: 11.5 us -> 19.3 us  [body(): lax.linalg.triangular_solve(factor, sketch_rows, left_side=False, lower=T...]
    psum x1, waiting for transfers between devices: 52 us -> 45.3 us  [body(): gram = lax.psum(local_gram, 'shard')]
    another operation x12, local copies, waits for them, and re-layouts: 7.74 us -> 13.8 us
  transfers between devices with their start and end apart: 3 -> 3, of which waited for: 3 -> 3; matrix products, arithmetic and copies ran while one was open for 0% -> 1% of each run, Pallas kernels for 0% -> 0%
where the time goes in v1:
time: 556 us; the launch traced here: 548 us
  waiting for transfers between devices  277 us (50%)
  other arithmetic  134 us (24%)
  matrix products  64.2 us (12%)
  local copies, waits for them, and re-layouts  55.2 us (10%)
  between operations  16.9 us (3%)
    all_gather x1, waiting for transfers between devices, summed_here(): pieces = lax.all_gather(x, axis)  163 us
    another operation x14, other arithmetic, body(): factor = jnp.linalg.cholesky(gram)  78.8 us
    reduce_scatter x1, waiting for transfers between devices, body(): lax.psum_scatter(partial_sum, 'shard', scatter_dimension=0, tiled=True)  68 us
    psum x1, waiting for transfers between devices, body(): gram = lax.psum(local_gram, 'shard')  45.3 us
    another operation x3, other arithmetic, body(): lax.linalg.triangular_solve(factor, sketch_rows, left_side=False, lower=T...  41.3 us
    unnamed x8, local copies, waits for them, and re-layouts  36.7 us
    another operation x7, matrix products, body(): lax.linalg.triangular_solve(factor, sketch_rows, left_side=False, lower=T...  19.3 us
    dot_general x1, matrix products, body(): partial = jnp.dot(g, table, preferred_element_type=jnp.float32)  16.8 us
  transfers between devices with their start and end apart: 3, of which 3 were waited for; matrix products, arithmetic and copies ran while one was open for 1% of the time, Pallas kernels for 0%

profile of v1, /device:TPU:0, one launch (start us, length us, event | category | flops | bytes accessed | tf_op | source)
XLA Modules:
  0.0 547.8 jit_solution(15405139574117030837)
XLA Ops:
  6.5 0.0 all-gather.3.cloned.1.call-start
  7.2 16.8 %fusion.27 = f32[2048,512]{0,1:T(8,128)} fusion(bf16[1,2048,3584]{2,1,0:T(8,128)(2,1)} %param.2, s32[]{:T(128)} %bitcast, s32[3584]{0:T(1024)S(1)} %add_multiply_fusion), kind=kOutput, calls=%fused_computation.27 | convolution fusion | flops 7540047872 | bytes 18888708 | tf_op jit(solution)/shard_map/dot_general | solution.py:37
  24.0 0.0 all-gather.3.cloned.1.call-update
  24.0 0.3 all-reduce.3.cloned.1.call-start
  24.3 163.3 %all-gather.3.cloned.1.call-done = f32[16384,512]{0,1:T(8,128)} async-done(((f32[2048,512]{0,1:T(8,128)}), f32[16384,512]{0,1:T(8,128)}) %all-gather.3.cloned.1.call-update) | async-done | bytes 33554448 | tf_op jit(solution)/shard_map/all_gather | solution.py:13
  187.6 32.5 %copy.16 = f32[64,8,8,2048]{3,2,1,0:T(8,128)S(1)} copy(f32[64,8,8,2048]{3,1,2,0:T(8,128)} %bitcast.82) | data formatting | bytes 67108864
  220.1 12.7 %bitcast_reduce_fusion = f32[2048,512]{0,1:T(8,128)} fusion(f32[64,8,8,2048]{3,2,1,0:T(8,128)S(1)} %copy.16), kind=kLoop, calls=%fused_computation.2 | loop fusion | flops 7340032 | bytes 37748736 | tf_op jit(solution)/shard_map/reduce_sum | solution.py:14
  232.7 10.2 %fusion.85 = f32[512,512]{0,1:T(8,128)} fusion(f32[2048,512]{0,1:T(8,128)} %bitcast_reduce_fusion), kind=kOutput, calls=%fused_computation.113 | convolution fusion | flops 6442450944 | bytes 5242880 | tf_op jit(solution)/shard_map/dot_general | solution.py:39
  243.0 0.0 all-reduce.3.cloned.1.call-update
  243.0 0.4 reduce-scatter.2.cloned.1.call-start
  243.5 3.1 fusion.81
  246.6 1.5 copy.13
  248.1 1.3 copy.14
  249.4 0.3 copy.15
  249.8 45.3 %all-reduce.3.cloned.1.call-done = f32[512,512]{0,1:T(8,128)} async-done(((f32[512,512]{0,1:T(8,128)}), f32[512,512]{0,1:T(8,128)}) %all-reduce.3.cloned.1.call-update) | async-done | bytes 1048592 | tf_op jit(solution)/shard_map/psum | solution.py:45
  295.1 1.6 copy.8
  296.6 1.4 fusion.53
  298.1 0.0 copy-start.1
  298.1 1.0 copy-done.1
  299.1 11.7 %cholesky.104 = f32[128,128]{1,0:T(8,128)S(1)} custom-call(f32[128,128]{1,0:T(8,128)S(1)} %cholesky.266), custom_call_target="Cholesky" | custom-call | tf_op jit(solution)/shard_map/jit(cholesky)/cholesky | solution.py:46
  310.8 9.8 %custom-call.30 = f32[1,128,128]{1,2,0:T(8,128)S(1)} custom-call(f32[1,128,128]{2,1,0:T(8,128)S(1)} %get-tuple-element.35), custom_call_target="InvertDiagBlocksLowerTriangular" | custom-call | tf_op jit(solution)/shard_map/jit(cholesky)/cholesky | solution.py:46
  320.7 0.1 cholesky.224
  320.8 1.2 constant_dynamic-update-slice_fusion.3
  322.0 1.3 convolution_subtract_fusion.2
  323.3 11.7 %cholesky.217 = f32[128,128]{1,0:T(8,128)S(1)} custom-call(f32[128,128]{1,0:T(8,128)S(1)} %cholesky.270), custom_call_target="Cholesky" | custom-call | tf_op jit(solution)/shard_map/jit(cholesky)/cholesky | solution.py:46
  335.1 10.0 %custom-call.31 = f32[1,128,128]{1,2,0:T(8,128)S(1)} custom-call(f32[1,128,128]{2,1,0:T(8,128)S(1)} %get-tuple-element.32), custom_call_target="InvertDiagBlocksLowerTriangular" | custom-call | tf_op jit(solution)/shard_map/jit(cholesky)/cholesky | solution.py:46
  345.0 0.3 convolution_dynamic-update-slice_fusion
  345.3 1.3 convolution_subtract_fusion.3
  346.6 11.7 %cholesky.238 = f32[128,128]{1,0:T(8,128)S(1)} custom-call(f32[128,128]{1,0:T(8,128)S(1)} %cholesky.275), custom_call_target="Cholesky" | custom-call | tf_op jit(solution)/shard_map/jit(cholesky)/cholesky | solution.py:46
  358.3 0.6 compare_reduce_fusion.1
  359.0 9.8 %custom-call.32 = f32[1,128,128]{1,2,0:T(8,128)S(1)} custom-call(f32[1,128,128]{2,1,0:T(8,128)S(1)} %get-tuple-element.29), custom_call_target="InvertDiagBlocksLowerTriangular" | custom-call | tf_op jit(solution)/shard_map/jit(cholesky)/cholesky | solution.py:46
  368.8 0.2 convolution_dynamic-update-slice_fusion.1
  369.0 1.2 convolution_subtract_fusion.4
  370.2 11.9 %cholesky.255 = f32[128,128]{1,0:T(8,128)S(1)} custom-call(f32[128,128]{1,0:T(8,128)S(1)} %convolution_subtract_fusion.4), custom_call_target="Cholesky" | custom-call | tf_op jit(solution)/shard_map/jit(cholesky)/cholesky | solution.py:46
  382.2 0.7 compare_reduce_fusion
  382.9 0.7 compare_reduce_fusion.2
  386.0 1.1 select_select_fusion
  387.2 13.8 %while.1 = (s32[]{:T(128)}, f32[512,512]{1,0:T(8,128)}, s32[4,2]{0,1:T(2,128)S(1)}, f32[4,128,128]{2,1,0:T(8,128)}, s32[]{:T(128)}) while((s32[]{:T(128)}, f32[512,512]{1,0:T(8,128)}, s32[4,2]{0,1:T(2,128)S(1)}, f32[4,128,128]{2,1,0:T(8,128)}, s32[]{:T(128)}) %tuple.32), condition=%wide.while_cond, body=%wide.while_body.sunk | while | flops 2 | bytes 132705 | solution.py:47
  387.2 0.1 constant_dynamic-slice_fusion.2
  387.3 0.5 fusion.94
  387.8 2.8 bitcast_dynamic-update-slice_fusion.2
  390.6 0.1 constant_dynamic-slice_fusion.2
  390.7 0.5 fusion.94
  391.3 2.8 bitcast_dynamic-update-slice_fusion.2
  394.1 0.1 constant_dynamic-slice_fusion.2
  394.2 0.5 fusion.94
  394.7 2.8 bitcast_dynamic-update-slice_fusion.2
  397.6 0.1 constant_dynamic-slice_fusion.2
  397.6 0.5 fusion.94
  398.2 2.8 bitcast_dynamic-update-slice_fusion.2
  400.9 40.1 %custom-call.33 = f32[4,128,128]{1,2,0:T(8,128)S(1)} custom-call(f32[4,128,128]{2,1,0:T(8,128)} %get-tuple-element.12), custom_call_target="InvertDiagBlocksLowerTriangular" | custom-call | tf_op jit(solution)/shard_map/triangular_solve | solution.py:47
  441.1 0.0 copy-start
  441.1 2.4 fusion.84
  443.5 2.7 convolution_subtract_fusion.1
  446.1 1.1 fusion.83
  447.2 0.0 copy-done
  447.2 4.5 convolution_subtract_fusion
  451.7 1.1 fusion.82
  452.8 6.5 %fusion.38 = f32[2048,128]{1,0:T(8,128)S(1)} fusion(f32[2048,128]{1,0:T(8,128)S(1)} %copy.15, f32[2048,128]{0,1:T(8,128)S(1)} %get-tuple-element.39, f32[2048,128]{0,1:T(8,128)S(1)} %get-tuple-element.41, f32[2048,128]{0,1:T(8,128)S(1)} %get-tuple-element.43, f32[512,512]{1,0:T(8,128)} %get-tuple-element.101), kind=kOutput, calls=%fused_computation.34 | convolution fusion | flops 1209794560 | bytes 5439488 | tf_op jit(solution)/shard_map/triangular_solve | solution.py:47
  459.4 1.1 convolution_convert_fusion
  460.4 12.4 %fusion.13 = bf16[512,1,3584]{2,0,1:T(8,128)(2,1)} fusion(bf16[1,2048,3584]{2,1,0:T(8,128)(2,1)} %param.2, bf16[2048,128]{0,1:T(8,128)(2,1)S(1)} %convolution_convert_fusion, bf16[2048,128]{0,1:T(8,128)(2,1)S(1)} %get-tuple-element.38, bf16[2048,128]{0,1:T(8,128)(2,1)S(1)} %get-tuple-element.40, bf16[2048,128]{0,1:T(8,128)(2,1)S(1)} %get-tuple-element.42), kind=kOutput, calls=%fused_computation.16 | convolution fusion | flops 7526416384 | bytes 20447232 | tf_op jit(solution)/shard_map/dot_general | solution.py:50
  472.8 0.0 reduce-scatter.2.cloned.1.call-update
  472.9 68.0 %reduce-scatter.2.cloned.1.call-done = bf16[128,1,3584]{2,0,1:T(8,128)(2,1)} async-done(((bf16[512,1,3584]{2,0,1:T(8,128)(2,1)}), bf16[128,1,3584]{2,0,1:T(8,128)(2,1)}) %reduce-scatter.2.cloned.1.call-update) | async-done | bytes 917520 | tf_op jit(solution)/shard_map/reduce_scatter | solution.py:53
  (11 shorter events, 0.2 us)
Async XLA Ops:
  6.5 181.0 %all-gather.3.cloned.1.call-start = ((), (), s32[]{:S(2)}) async-start(), calls=%async_computation.3 | async-start | bytes 37748736 | tf_op jit(solution)/shard_map/all_gather | solution.py:13
  24.0 271.0 %all-reduce.3.cloned.1.call-start = ((), (), s32[]{:S(2)}) async-start(), calls=%async_computation.1 | async-start | bytes 2097152 | tf_op jit(solution)/shard_map/psum | solution.py:45
  243.0 297.8 %reduce-scatter.2.cloned.1.call-start = ((), (), s32[]{:S(2)}) async-start(), calls=%async_computation.2 | async-start | bytes 4587520 | tf_op jit(solution)/shard_map/reduce_scatter | solution.py:53
  298.1 1.0 copy-start.1
  441.1 6.2 %copy-start = (f32[2048,128]{1,0:T(8,128)S(1)}, f32[2048,128]{1,0:T(8,128)}, u32[]{:S(2)}) copy-start(f32[2048,128]{1,0:T(8,128)} %copy.14) | copy-start | bytes 3145732
Sparse Core Ops, SparseCore 0:
  24.1 163.3 all-gather.2
  243.1 51.8 all-reduce.2
  473.0 67.8 reduce-scatter.1
